TPU v7x, 256 devices: a whole 4x4x8 slice. The times are simulated.
256 devices in a mesh: az: 16 (over z_lo, x, core), tile: 16 (over y, z_hi).
Axes of the slice: x: 4, y: 4, z: 8 (z_hi: 4, z_lo: 2; z = z_hi * 2 + z_lo), core: 2. Of those that a mesh axis runs over, the one named last changes fastest.
Arguments:
- image: float32 [2, 8192, 2048], P(None, 'tile', 'az'), may hold values from -6 to 6
- tv_dual: float32 [2, 2, 8192, 2048], P(None, None, 'tile', 'az'), may hold values from -3 to 3
- data_dual: float32 [2, 1024, 64, 128], P(None, 'az', 'tile'), may hold values from -3 to 3
- echoes: bfloat16 [2, 1024, 64, 128], P(None, 'az', 'tile'), may hold values from -6 to 6
- row_steer: bfloat16 [2, 1024, 32, 256], P(None, None, 'tile'), may hold values from -0.375 to 0.375
- col_steer: float32 [2, 1024, 32, 16], P(None, None, 'tile'), may hold values from -1.5 to 1.5
- kernels: bfloat16 [8, 128, 128], replicated, may hold values from -0.5 to 0.5
- footprint: int32 [32, 16, 6], P(None, 'az'), may hold values from 0 to 63
- phase: int32 [32, 16, 6], P(None, 'az'), may hold values from 0 to 7
- aperture: int32 [1024], P('az'), may hold values from 0 to 1, as said below
Outputs:
- image_new: float32 [2, 8192, 2048], P(None, 'tile', 'az')
- tv_new: float32 [2, 2, 8192, 2048], P(None, None, 'tile', 'az')
- dual_new: float32 [2, 1024, 64, 128], P(None, 'az', 'tile')
Inputs may be any that keep to these rules, and one draw needn't show every extreme that they name: 0 inside up to three gaps of 64 consecutive pulses each (wrapping around the aperture), 1 elsewhere.
All inputs are finite; a program needn't handle non-finite values.
Results may differ from a plain program's by a relative error of at most 0.0025.
The roundings to bfloat16 on the way count: a program that leaves them out, or rounds other values in their place, can miss the bound.
Values may be sent and summed in bfloat16 or wider, within the bound.
No kernel may reach another device: no remote copies, remote signals or barrier semaphores. Data moves between devices by JAX's collectives and lax.ppermute only.
A program may use at most 64 MiB of HBM per device.

v0:
```python
import jax
import jax.numpy as jnp
from jax import lax
from jax.sharding import PartitionSpec as P

dual_step = 0.5
primal_step = 0.25
edge_limit = 1.5


def padded_2(block, sides, width):
    for axis, dim in sides:
        count = lax.axis_size(axis)
        forward = [(i, i + 1) for i in range(count - 1)]
        backward = [(target, source) for source, target in forward]
        low = lax.ppermute(
            lax.slice_in_dim(block, block.shape[dim] - width, None, axis=dim), axis, forward
        )
        high = lax.ppermute(lax.slice_in_dim(block, 0, width, axis=dim), axis, backward)
        block = jnp.concatenate([low, block, high], axis=dim)
    return block


def on_device(
    image, tv_dual, data_dual, echoes, row_steer, col_steer, kernels, footprint, phase, aperture
):
    highest = lax.Precision.HIGHEST
    az_index = lax.axis_index("az")
    tile_index = lax.axis_index("tile")
    az_count = lax.axis_size("az")
    tile_count = lax.axis_size("tile")
    strip_rows = image.shape[1]
    columns = image.shape[2]
    tiles_dev = row_steer.shape[2]
    tile_rows = row_steer.shape[3]
    rows_dev = data_dual.shape[2]
    range_rows = rows_dev * tile_count
    foot_block = footprint[:, 0, :]
    phase_block = phase[:, 0, :]
    foot_mine = lax.dynamic_slice_in_dim(foot_block, tile_index * tiles_dev, tiles_dev, 0)
    phase_mine = lax.dynamic_slice_in_dim(phase_block, tile_index * tiles_dev, tiles_dev, 0)
    steer_re = row_steer[0]
    steer_im = row_steer[1]
    col_mine = lax.dynamic_slice_in_dim(col_steer, az_index, 1, 3)[..., 0]
    image_b = image.astype(jnp.bfloat16).reshape(2, tiles_dev, tile_rows, columns)
    part_sre = steer_re
    part_sim = steer_im
    weight_re = col_mine[0][..., None]
    weight_im = col_mine[1][..., None]
    prod_re = jnp.einsum("pjh,jhu->pju", part_sre, image_b[0], preferred_element_type=jnp.float32)
    prod_re = prod_re - jnp.einsum(
        "pjh,jhu->pju", part_sim, image_b[1], preferred_element_type=jnp.float32
    )
    prod_im = jnp.einsum("pjh,jhu->pju", part_sre, image_b[1], preferred_element_type=jnp.float32)
    prod_im = prod_im + jnp.einsum(
        "pjh,jhu->pju", part_sim, image_b[0], preferred_element_type=jnp.float32
    )
    real_part = weight_re * prod_re - weight_im * prod_im
    imag_part = weight_re * prod_im + weight_im * prod_re
    summed = lax.psum_scatter(
        jnp.stack([real_part, imag_part], axis=0), "az", scatter_dimension=1, tiled=True
    )
    projection_b = jnp.transpose(summed, (2, 1, 0, 3)).astype(jnp.bfloat16)
    all_proj = lax.all_gather(projection_b, "tile", axis=0, tiled=True)
    phase_ids = jnp.arange(kernels.shape[0], dtype=jnp.int32)
    my_rows = tile_index * rows_dev + jnp.arange(rows_dev, dtype=jnp.int32)
    hits = (foot_block[:, :, None, None] == my_rows[None, None, :, None]) & (
        phase_block[:, :, None, None] == phase_ids[None, None, None, :]
    )
    counts = jnp.sum(hits.astype(jnp.int32), axis=1).astype(jnp.bfloat16)
    grouped = jnp.einsum("jkq,jpcu->kqpcu", counts, all_proj, preferred_element_type=jnp.float32)
    forward = jnp.einsum("kqpcu,quv->cpkv", grouped, kernels.astype(jnp.float32), precision=highest)
    kern_mine = kernels[phase_mine]
    live = (aperture == 1)[None, :, None, None]
    dual_new = jnp.where(
        live,
        (data_dual + dual_step * (forward - echoes.astype(jnp.float32))) / (1.0 + dual_step),
        0.0,
    )
    dual_b = dual_new.astype(jnp.bfloat16)
    all_rows = lax.all_gather(dual_b, "tile", axis=2, tiled=True)
    chosen = jnp.take(all_rows, foot_mine, axis=2)
    back = jnp.einsum("cpjfv,jfuv->cjpu", chosen, kern_mine, preferred_element_type=jnp.float32)
    back_b = back.astype(jnp.bfloat16)
    piece = lax.all_gather(back_b, "az", axis=2, tiled=True)
    weight_re = col_mine[0].T[..., None]
    weight_im = col_mine[1].T[..., None]
    back_re = piece[0].astype(jnp.float32)
    back_im = piece[1].astype(jnp.float32)
    mixed_re = (weight_re * back_re + weight_im * back_im).astype(jnp.bfloat16)
    mixed_im = (weight_re * back_im - weight_im * back_re).astype(jnp.bfloat16)
    part_sre = steer_re
    part_sim = steer_im
    grad_re = jnp.einsum("pjh,jpu->jhu", part_sre, mixed_re, preferred_element_type=jnp.float32)
    grad_re = grad_re + jnp.einsum(
        "pjh,jpu->jhu", part_sim, mixed_im, preferred_element_type=jnp.float32
    )
    grad_im = jnp.einsum("pjh,jpu->jhu", part_sre, mixed_im, preferred_element_type=jnp.float32)
    grad_im = grad_im - jnp.einsum(
        "pjh,jpu->jhu", part_sim, mixed_re, preferred_element_type=jnp.float32
    )
    adjoint = jnp.stack([grad_re, grad_im])
    adjoint = adjoint.reshape(2, strip_rows, columns)
    stacked = jnp.concatenate([image, tv_dual.reshape(4, strip_rows, columns)], axis=0)
    padded = padded_2(stacked, (("az", 2), ("tile", 1)), 1)
    image_pad = padded[:2]
    dual_pad = padded[2:].reshape(2, 2, strip_rows + 2, columns + 2)
    total_rows = tile_count * strip_rows
    total_cols = az_count * columns
    global_row = tile_index * strip_rows - 1 + jnp.arange(strip_rows + 1, dtype=jnp.int32)
    global_col = az_index * columns - 1 + jnp.arange(columns + 1, dtype=jnp.int32)
    centre = image_pad[:, : strip_rows + 1, : columns + 1]
    grad_rows = image_pad[:, 1 : strip_rows + 2, : columns + 1] - centre
    grad_rows = jnp.where((global_row < total_rows - 1)[None, :, None], grad_rows, 0.0)
    grad_cols = image_pad[:, : strip_rows + 1, 1 : columns + 2] - centre
    grad_cols = jnp.where((global_col < total_cols - 1)[None, None, :], grad_cols, 0.0)
    moved = dual_pad[:, :, : strip_rows + 1, : columns + 1] + dual_step * jnp.stack(
        [grad_rows, grad_cols]
    )
    magnitude = jnp.sqrt(jnp.sum(moved * moved, axis=(0, 1)))
    projected = moved / jnp.maximum(1.0, magnitude / edge_limit)
    inside = (global_row >= 0)[:, None] & (global_col >= 0)[None, :]
    projected = jnp.where(inside[None, None], projected, 0.0)
    rows_part = jnp.where((global_row < total_rows - 1)[None, :, None], projected[0], 0.0)
    cols_part = jnp.where((global_col < total_cols - 1)[None, None, :], projected[1], 0.0)
    divergence = (
        rows_part[:, 1:, 1:] - rows_part[:, :-1, 1:] + cols_part[:, 1:, 1:] - cols_part[:, 1:, :-1]
    )
    image_new = image - primal_step * (adjoint - divergence)
    tv_new = projected[:, :, 1:, 1:]
    return (image_new, tv_new, dual_new)


def solution(mesh):
    in_specs = (
        P(None, "tile", "az"),
        P(None, None, "tile", "az"),
        P(None, "az", "tile", None),
        P(None, "az", "tile", None),
        P(None, None, "tile", None),
        P(None, None, "tile", None),
        P(),
        P(None, "az", None),
        P(None, "az", None),
        P("az"),
    )
    out_specs = (P(None, "tile", "az"), P(None, None, "tile", "az"), P(None, "az", "tile", None))
    return jax.shard_map(
        on_device, mesh=mesh, in_specs=in_specs, out_specs=out_specs, check_vma=False
    )
```

profile of v0, /device:TPU:1, one launch (start us, length us, event | category | flops | bytes accessed | tf_op | source)
XLA Modules:
  0.0 264.6 jit_solution(16992743149203517460)
XLA Ops:
  7.3 2.7 %fusion.64 = (bf16[1,1024,2,256]{3,2,1,0:T(2,128)(2,1)S(1)}, bf16[1,1024,2,256]{3,2,1,0:T(2,128)(2,1)S(1)}) fusion(bf16[2,1024,2,256]{3,2,1,0:T(2,128)(2,1)} %param.14), kind=kLoop, calls=%fused_computation.122 | loop fusion | bytes 4194304 | tf_op jit(solution)/shard_map/slice | solution.py:43
  10.1 0.5 fusion.43
  10.6 0.4 copy-done.8
  11.0 1.5 fusion.44
  12.4 0.9 constant_dynamic-slice_fusion
  13.4 0.5 fusion.2
  13.9 0.7 copy-done.10
  14.6 0.6 subtract_bitcast_fusion
  15.2 0.2 pad_maximum_fusion.5
  15.4 2.3 copy.117
  17.8 66.7 %all-reduce.2 = bf16[2,1024,2,128]{3,2,0,1:T(2,128)(2,1)S(1)} all-reduce(f32[2,1024,2,128]{3,2,0,1:T(2,128)} %copy.117), channel_id=2, replica_groups=mesh['az'=16,'tile'=16] {'az'}, use_global_device_ids=true, to_apply=%region_1.0.clone | all-reduce | flops 524288 | bytes 3145728
  84.5 0.6 dynamic-slice.2
  85.8 0.6 copy.118
  86.7 56.0 %all-gather.4.cloned.1.call-done = bf16[32,64,2,128]{3,1,2,0:T(8,128)(2,1)} async-done(((bf16[2,64,2,128]{3,1,2,0:T(8,128)(2,1)}), bf16[32,64,2,128]{3,1,2,0:T(8,128)(2,1)}) %all-gather.4.cloned.1.call-update) | async-done | bytes 1048592 | tf_op jit(solution)/shard_map/all_gather | solution.py:64
  142.7 2.0 fusion.38
  144.8 2.3 fusion.66
  147.2 1.6 slice_maximum_fusion
  148.8 1.9 copy.132
  150.7 5.0 %collective-permute-start = (f32[6,512,1]{1,2,0:T(1,128)S(1)}, f32[6,512,1]{1,2,0:T(1,128)S(1)}, u32[]{:S(2)}, u32[]{:S(2)}) collective-permute-start(f32[6,512,1]{1,2,0:T(1,128)S(1)} %copy.132), channel_id=1, source_target_pairs={{0,16},{16,32},{32,48},{48,64},{64,80},{80,96},{96,112},{112,128},... | collective-permute-start | bytes 36872 | tf_op jit(solution)/shard_map/ppermute | solution.py:16
  155.7 0.5 copy.133
  156.1 1.9 collective-permute-start.1
  158.6 1.4 gather_fusion
  160.0 0.5 copy.134
  160.5 0.6 collective-permute-done.1
  161.2 0.5 copy.135
  161.7 0.9 pad_maximum_fusion.16
  162.5 2.0 collective-permute-start.2
  164.5 1.5 collective-permute-start.3
  166.0 38.9 %all-gather.6.cloned.1.call-done = bf16[2,64,64,128]{3,1,0,2:T(8,128)(2,1)} async-done(((bf16[2,64,4,128]{3,1,0,2:T(8,128)(2,1)}), bf16[2,64,64,128]{3,1,0,2:T(8,128)(2,1)}) %all-gather.6.cloned.1.call-update) | async-done | bytes 2097168 | tf_op jit(solution)/shard_map/all_gather | solution.py:81
  204.9 2.9 %gather_fusion.1 = bf16[12,2,64,128]{3,2,1,0:T(8,128)(2,1)} fusion(bf16[2,64,64,128]{3,1,0,2:T(8,128)(2,1)} %all-gather.6.cloned.1.call-done, s32[1024]{0:T(1024)S(1)} %pad_clamp_fusion), kind=kCustom, calls=%fused_computation.1 | custom fusion | bytes 786480 | tf_op jit(solution)/shard_map/jit(_take)/gather | solution.py:82
  207.8 2.1 fusion.25
  210.1 2.2 pad_maximum_fusion
  212.3 0.6 fusion.30
  213.0 1.0 fusion.33
  213.9 0.4 multiply_reduce_fusion
  214.3 0.2 multiply_maximum_fusion
  214.5 0.4 divide_select_fusion
  214.9 1.3 slice.128
  216.2 1.2 fusion.27
  217.4 0.9 copy.136
  218.3 25.4 %all-gather.8.cloned.1.call-done = bf16[2,2,1024,128]{3,2,0,1:T(8,128)(2,1)} async-done(((bf16[2,2,64,128]{3,2,0,1:T(8,128)(2,1)}), bf16[2,2,1024,128]{3,2,0,1:T(8,128)(2,1)}) %all-gather.8.cloned.1.call-update) | async-done | bytes 1048592 | tf_op jit(solution)/shard_map/all_gather | solution.py:85
  243.7 2.4 fusion.42
  246.2 2.0 fusion.7
  248.1 1.8 copy.128
  249.9 2.4 fusion.41
  252.3 2.0 fusion.8
  254.3 1.1 copy.131
  255.4 2.7 %fusion.47 = f32[2,512,128]{2,1,0:T(8,128)} fusion(f32[2,512,128]{2,1,0:T(8,128)S(1)} %copy-done.5, f32[2,513,129]{2,1,0:T(8,128)} %get-tuple-element.21, f32[2,513,129]{2,1,0:T(8,128)S(1)} %get-tuple-element.20, f32[1,512,128]{2,1,0:T(8,128)S(1)} %bitcast.164, f32[1,512,128]{2,1,0:T(8,128)S(1)} %bitcast.163), kind=kLoop, calls=%fused_computation.75 | loop fusion | flops 917504 | bytes 3670016 | tf_op jit(solution)/shard_map/sub | solution.py:129
  (73 shorter events, 1.2 us)
Async XLA Ops:
  7.2 137.6 %copy-start = (bf16[8,128,128]{2,1,0:T(8,128)(2,1)S(1)}, bf16[8,128,128]{2,1,0:T(8,128)(2,1)}, u32[]{:S(2)}) copy-start(bf16[8,128,128]{2,1,0:T(8,128)(2,1)} %param.16) | copy-start | bytes 786436
  7.2 135.5 %all-gather.4.cloned.1.call-start = ((), (), s32[]{:S(2)}) async-start(), calls=%async_computation | async-start | bytes 1114112 | tf_op jit(solution)/shard_map/all_gather | solution.py:64
  7.2 2.8 %copy-start.3 = (f32[2,512,128]{2,1,0:T(8,128)S(1)}, f32[2,512,128]{2,1,0:T(8,128)}, u32[]{:S(2)}) copy-start(f32[2,512,128]{2,1,0:T(8,128)} %param.10) | copy-start | bytes 1572868
  10.0 1.0 copy-start.8
  10.0 3.8 %copy-start.6 = (bf16[1,1024,2,256]{3,2,1,0:T(2,128)(2,1)}, bf16[1,1024,2,256]{3,2,1,0:T(2,128)(2,1)S(1)}, u32[]{:S(2)}) copy-start(bf16[1,1024,2,256]{3,2,1,0:T(2,128)(2,1)S(1)} %get-tuple-element.24) | copy-start | bytes 3145732
  13.4 1.2 copy-start.10
  17.7 66.8 %copy-start.20 = (u32[256]{0:T(256)S(1)}, u32[256]{0:T(256)}, u32[]{:S(2)}) copy-start(u32[256]{0:T(256)} %constant.75) | copy-start | bytes 3076
  17.7 68.8 %copy-start.15 = (s32[32,1,6]{0,1,2:T(1,128)S(1)}, s32[32,1,6]{0,1,2:T(1,128)}, u32[]{:S(2)}) copy-start(s32[32,1,6]{0,1,2:T(1,128)} %param.17) | copy-start | bytes 2308
  17.7 68.8 %copy-start.16 = (s32[32,1,6]{0,1,2:T(1,128)S(1)}, s32[32,1,6]{0,1,2:T(1,128)}, u32[]{:S(2)}) copy-start(s32[32,1,6]{0,1,2:T(1,128)} %param.18) | copy-start | bytes 2308
  17.7 69.0 %copy-start.19 = (s32[64]{0:T(128)S(1)}, s32[64]{0:T(128)}, u32[]{:S(2)}) copy-start(s32[64]{0:T(128)} %param.19) | copy-start | bytes 772
  86.5 118.4 %all-gather.6.cloned.1.call-start = ((), (), s32[]{:S(2)}) async-start(), calls=%async_computation.1 | async-start | bytes 2228224 | tf_op jit(solution)/shard_map/all_gather | solution.py:81
  86.7 58.0 %copy-start.13 = (f32[2,64,4,128]{3,2,1,0:T(4,128)S(1)}, f32[2,64,4,128]{3,2,1,0:T(4,128)}, u32[]{:S(2)}) copy-start(f32[2,64,4,128]{3,2,1,0:T(4,128)} %param.12) | copy-start | bytes 786436
  86.7 58.0 %copy-start.14 = (bf16[2,64,4,128]{3,2,1,0:T(4,128)(2,1)S(1)}, bf16[2,64,4,128]{3,2,1,0:T(4,128)(2,1)}, u32[]{:S(2)}) copy-start(bf16[2,64,4,128]{3,2,1,0:T(4,128)(2,1)} %param.13) | copy-start | bytes 393220
  144.8 2.4 copy-start.1
  147.1 96.6 %all-gather.8.cloned.1.call-start = ((), (), s32[]{:S(2)}) async-start(), calls=%async_computation.2 | async-start | bytes 1114112 | tf_op jit(solution)/shard_map/all_gather | solution.py:85
  150.7 9.3 %collective-permute-start = (f32[6,512,1]{1,2,0:T(1,128)S(1)}, f32[6,512,1]{1,2,0:T(1,128)S(1)}, u32[]{:S(2)}, u32[]{:S(2)}) collective-permute-start(f32[6,512,1]{1,2,0:T(1,128)S(1)} %copy.132), channel_id=1, source_target_pairs={{0,16},{16,32},{32,48},{48,64},{64,80},{80,96},{96,112},{112,128},... | collective-permute-start | bytes 36872 | tf_op jit(solution)/shard_map/ppermute | solution.py:16
  156.1 5.0 %collective-permute-start.1 = (f32[6,512,1]{1,2,0:T(1,128)S(1)}, f32[6,512,1]{1,2,0:T(1,128)S(1)}, u32[]{:S(2)}, u32[]{:S(2)}) collective-permute-start(f32[6,512,1]{1,2,0:T(1,128)S(1)} %copy.133), channel_id=1, source_target_pairs={{16,0},{32,16},{48,32},{64,48},{80,64},{96,80},{112,96},{128,112},... | collective-permute-start | bytes 36872 | tf_op jit(solution)/shard_map/ppermute | solution.py:19
  162.5 47.5 %collective-permute-start.2 = (f32[6,1,130]{2,1,0:T(1,128)S(1)}, f32[6,1,130]{2,1,0:T(1,128)S(1)}, u32[]{:S(2)}, u32[]{:S(2)}) collective-permute-start(f32[6,1,130]{2,1,0:T(1,128)S(1)} %get-tuple-element.19), channel_id=1, source_target_pairs={{0,1},{1,2},{2,3},{3,4},{4,5},{5,6},{6,7},{7,8},{8,9},{9,10},{10,1... | collective-permute-start | bytes 9368 | tf_op jit(solution)/shard_map/ppermute | solution.py:16
  164.5 45.6 %collective-permute-start.3 = (f32[6,1,130]{2,1,0:T(1,128)S(1)}, f32[6,1,130]{2,1,0:T(1,128)S(1)}, u32[]{:S(2)}, u32[]{:S(2)}) collective-permute-start(f32[6,1,130]{2,1,0:T(1,128)S(1)} %get-tuple-element.18), channel_id=1, source_target_pairs={{1,0},{2,1},{3,2},{4,3},{5,4},{6,5},{7,6},{8,7},{9,8},{10,9},{11,1... | collective-permute-start | bytes 9368 | tf_op jit(solution)/shard_map/ppermute | solution.py:19
  210.0 2.3 copy-start.2
  210.0 2.3 copy-start.4
  216.2 1.2 copy-start.12
  216.2 27.5 %copy-start.9 = (bf16[1,1024,2,256]{3,2,1,0:T(2,128)(2,1)S(1)}, bf16[1,1024,2,256]{3,2,1,0:T(2,128)(2,1)}, u32[]{:S(2)}) copy-start(bf16[1,1024,2,256]{3,2,1,0:T(2,128)(2,1)} %copy-done.8) | copy-start | bytes 3145732
  243.7 2.5 copy-start.7
  243.7 2.5 copy-start.17
  249.9 2.4 copy-start.18
  252.3 3.1 %copy-start.5 = (f32[2,512,128]{2,1,0:T(8,128)S(1)}, f32[2,512,128]{2,1,0:T(8,128)}, u32[]{:S(2)}) copy-start(f32[2,512,128]{2,1,0:T(8,128)} %param.10) | copy-start | bytes 1572868
  252.3 3.1 %copy-start.11 = (f32[2,256,128]{2,1,0:T(8,128)S(1)}, f32[2,256,128]{2,1,0:T(8,128)}, u32[]{:S(2)}) copy-start(f32[2,256,128]{2,1,0:T(8,128)} %copy.128) | copy-start | bytes 786436
Sparse Core Ops, SparseCore 0:
  86.6 56.0 all-gather.3
  147.2 57.5 all-gather.5
  210.0 33.6 all-gather.7
where the time goes:
time: 265 us
  waiting for transfers between devices  121 us (46%)
  blocking collectives  66.7 us (25%)
  local copies, waits for them, and re-layouts  21.7 us (8%)
  matrix products  18.1 us (7%)
  between operations  15 us (6%)
  other arithmetic  11.7 us (4%)
  starting transfers between devices  10.4 us (4%)
    unnamed x1, blocking collectives  66.7 us
    all_gather x1, waiting for transfers between devices, on_device(): all_proj = lax.all_gather(projection_b, 'tile', axis=0, tiled=True)  56 us
    all_gather x1, waiting for transfers between devices, on_device(): all_rows = lax.all_gather(dual_b, 'tile', axis=2, tiled=True)  38.9 us
    all_gather x1, waiting for transfers between devices, on_device(): piece = lax.all_gather(back_b, 'az', axis=2, tiled=True)  25.4 us
    ppermute x2, starting transfers between devices, padded_2(): lax.ppermute(lax.slice_in_dim(block, block.shape[dim] - width, None, axis...  6.92 us
  transfers between devices with their start and end apart: 7, of which 4 were waited for; matrix products, arithmetic and copies ran while one was open for 8% of the time, Pallas kernels for 0%

commit v1 on v0

--- a/solution.py
+++ b/solution.py
@@ -61,7 +61,9 @@
         jnp.stack([real_part, imag_part], axis=0), "az", scatter_dimension=1, tiled=True
     )
     projection_b = jnp.transpose(summed, (2, 1, 0, 3)).astype(jnp.bfloat16)
-    all_proj = lax.all_gather(projection_b, "tile", axis=0, tiled=True)
+    all_proj = jnp.concatenate(
+        lax.all_to_all(jnp.stack([projection_b] * lax.axis_size("tile")), "tile", 0, 0), axis=0
+    )
     phase_ids = jnp.arange(kernels.shape[0], dtype=jnp.int32)
     my_rows = tile_index * rows_dev + jnp.arange(rows_dev, dtype=jnp.int32)
     hits = (foot_block[:, :, None, None] == my_rows[None, None, :, None]) & (

time: 265 us -> 249 us (0.940)
  waiting for transfers between devices: 121 us -> 92.2 us
  starting transfers between devices: 10.4 us -> 21.1 us
  local copies, waits for them, and re-layouts: 21.7 us -> 24.5 us
    all_gather x1 -> x0, waiting for transfers between devices: 56 us -> none  [on_device(): all_proj = lax.all_gather(projection_b, 'tile', axis=0, tiled=True)]
    all_to_all x0 -> x1, waiting for transfers between devices: none -> 25.3 us  [on_device(): lax.all_to_all(jnp.stack([projection_b] * lax.axis_size('tile')), 'tile',...]
    all_to_all x0 -> x1, starting transfers between devices: none -> 10 us  [on_device(): lax.all_to_all(jnp.stack([projection_b] * lax.axis_size('tile')), 'tile',...]
    ppermute x2, starting transfers between devices: 3.39 us -> 6.07 us  [padded_2(): lax.ppermute(lax.slice_in_dim(block, 0, width, axis=dim), axis, backward)]
  transfers between devices with their start and end apart: 7 -> 7, of which waited for: 4 -> 3; matrix products, arithmetic and copies ran while one was open for 8% -> 9% of each run, Pallas kernels for 0% -> 0%
where the time goes in v1:
time: 249 us; the launch traced here: 248 us
  waiting for transfers between devices  92.2 us (37%)
  blocking collectives  66.7 us (27%)
  local copies, waits for them, and re-layouts  24.5 us (10%)
  starting transfers between devices  21.1 us (8%)
  matrix products  16.5 us (7%)
  between operations  15.3 us (6%)
  other arithmetic  11.7 us (5%)
    unnamed x1, blocking collectives  66.7 us
    all_gather x1, waiting for transfers between devices, on_device(): all_rows = lax.all_gather(dual_b, 'tile', axis=2, tiled=True)  41.5 us
    all_gather x1, waiting for transfers between devices, on_device(): piece = lax.all_gather(back_b, 'az', axis=2, tiled=True)  25.4 us
    all_to_all x1, waiting for transfers between devices, on_device(): lax.all_to_all(jnp.stack([projection_b] * lax.axis_size('tile')), 'tile',...  25.3 us
    all_to_all x1, starting transfers between devices, on_device(): lax.all_to_all(jnp.stack([projection_b] * lax.axis_size('tile')), 'tile',...  10 us
    ppermute x2, starting transfers between devices, padded_2(): lax.ppermute(lax.slice_in_dim(block, 0, width, axis=dim), axis, backward)  6.07 us
  transfers between devices with their start and end apart: 7, of which 3 were waited for; matrix products, arithmetic and copies ran while one was open for 9% of the time, Pallas kernels for 0%

profile of v1, /device:TPU:1, one launch (start us, length us, event | category | flops | bytes accessed | tf_op | source)
XLA Modules:
  0.0 248.0 jit_solution(8014998258224987105)
XLA Ops:
  7.2 2.7 %fusion.62 = (bf16[1,1024,2,256]{3,2,1,0:T(2,128)(2,1)S(1)}, bf16[1,1024,2,256]{3,2,1,0:T(2,128)(2,1)S(1)}) fusion(bf16[2,1024,2,256]{3,2,1,0:T(2,128)(2,1)} %param.14), kind=kLoop, calls=%fused_computation.120 | loop fusion | bytes 4194304 | tf_op jit(solution)/shard_map/slice | solution.py:43
  10.1 0.5 fusion.40
  10.6 0.4 copy-done.8
  11.0 1.5 fusion.41
  12.4 0.9 constant_dynamic-slice_fusion
  13.3 0.5 fusion.2
  13.8 0.7 copy-done.10
  14.6 0.6 subtract_bitcast_fusion
  15.4 2.3 copy.118
  17.7 66.7 %all-reduce.2 = bf16[2,1024,2,128]{3,2,0,1:T(2,128)(2,1)S(1)} all-reduce(f32[2,1024,2,128]{3,2,0,1:T(2,128)} %copy.118), channel_id=2, replica_groups=mesh['az'=16,'tile'=16] {'az'}, use_global_device_ids=true, to_apply=%region_1.0.clone | all-reduce | flops 524288 | bytes 3145728
  84.5 0.6 dynamic-slice.2
  85.8 1.8 stack.23
  87.6 10.0 %all-to-all-start = ((bf16[16,2,64,2,128]{4,1,3,2,0:T(2,128)(2,1)}), bf16[16,2,64,2,128]{4,1,3,2,0:T(2,128)(2,1)S(1)}, u32[]{:S(2)}, u32[]{:S(2)}) async-start(bf16[16,2,64,2,128]{4,1,3,2,0:T(2,128)(2,1)} %stack.23), calls=%async_computation | async-start | bytes 2097152 | tf_op jit(solution)/shard_map/all_to_all | solution.py:65
  97.9 25.3 %all-to-all-done = bf16[16,2,64,2,128]{4,1,3,2,0:T(2,128)(2,1)S(1)} async-done(((bf16[16,2,64,2,128]{4,1,3,2,0:T(2,128)(2,1)}), bf16[16,2,64,2,128]{4,1,3,2,0:T(2,128)(2,1)S(1)}, u32[]{:S(2)}, u32[]{:S(2)}) %all-to-all-start) | async-done | bytes 1048608 | tf_op jit(solution)/shard_map/all_to_all | solution.py:65
  123.1 1.1 copy.119
  124.3 0.4 fusion.50
  124.7 0.5 copy-done.13
  125.3 2.3 fusion.64
  127.7 1.6 slice_maximum_fusion
  129.3 1.9 copy.132
  131.2 2.8 %collective-permute-start = (f32[6,512,1]{1,2,0:T(1,128)S(1)}, f32[6,512,1]{1,2,0:T(1,128)S(1)}, u32[]{:S(2)}, u32[]{:S(2)}) collective-permute-start(f32[6,512,1]{1,2,0:T(1,128)S(1)} %copy.132), channel_id=1, source_target_pairs={{0,16},{16,32},{32,48},{48,64},{64,80},{80,96},{96,112},{112,128},... | collective-permute-start | bytes 36872 | tf_op jit(solution)/shard_map/ppermute | solution.py:16
  134.0 0.5 copy.133
  134.5 4.6 %collective-permute-start.1 = (f32[6,512,1]{1,2,0:T(1,128)S(1)}, f32[6,512,1]{1,2,0:T(1,128)S(1)}, u32[]{:S(2)}, u32[]{:S(2)}) collective-permute-start(f32[6,512,1]{1,2,0:T(1,128)S(1)} %copy.133), channel_id=1, source_target_pairs={{16,0},{32,16},{48,32},{64,48},{80,64},{96,80},{112,96},{128,112},... | collective-permute-start | bytes 36872 | tf_op jit(solution)/shard_map/ppermute | solution.py:19
  139.7 1.4 gather_fusion
  141.1 0.5 copy.134
  141.6 0.5 copy.135
  142.1 0.9 pad_maximum_fusion.16
  142.9 2.0 collective-permute-start.2
  145.0 1.5 collective-permute-start.3
  146.5 41.5 %all-gather.3.cloned.1.call-done = bf16[2,64,64,128]{3,1,0,2:T(8,128)(2,1)} async-done(((bf16[2,64,4,128]{3,1,0,2:T(8,128)(2,1)}), bf16[2,64,64,128]{3,1,0,2:T(8,128)(2,1)}) %all-gather.3.cloned.1.call-update) | async-done | bytes 2097168 | tf_op jit(solution)/shard_map/all_gather | solution.py:83
  188.0 2.9 %gather_fusion.1 = bf16[12,2,64,128]{3,2,1,0:T(8,128)(2,1)} fusion(bf16[2,64,64,128]{3,1,0,2:T(8,128)(2,1)} %all-gather.3.cloned.1.call-done, s32[1024]{0:T(1024)S(1)} %pad_clamp_fusion), kind=kCustom, calls=%fused_computation.1 | custom fusion | bytes 786480 | tf_op jit(solution)/shard_map/jit(_take)/gather | solution.py:84
  190.9 2.1 fusion.25
  193.2 2.2 pad_maximum_fusion
  195.5 0.6 fusion.30
  196.1 1.0 fusion.33
  197.1 0.4 multiply_reduce_fusion
  197.6 0.4 divide_select_fusion
  198.0 1.3 slice.128
  199.3 1.2 fusion.27
  200.5 0.9 copy.136
  201.4 25.4 %all-gather.5.cloned.1.call-done = bf16[2,2,1024,128]{3,2,0,1:T(8,128)(2,1)} async-done(((bf16[2,2,64,128]{3,2,0,1:T(8,128)(2,1)}), bf16[2,2,1024,128]{3,2,0,1:T(8,128)(2,1)}) %all-gather.5.cloned.1.call-update) | async-done | bytes 1048592 | tf_op jit(solution)/shard_map/all_gather | solution.py:87
  226.8 2.4 fusion.39
  229.3 2.0 fusion.7
  231.2 1.8 copy.128
  233.0 2.4 fusion.38
  235.5 2.0 fusion.8
  237.4 1.1 copy.131
  238.5 2.7 %fusion.44 = f32[2,512,128]{2,1,0:T(8,128)} fusion(f32[2,512,128]{2,1,0:T(8,128)S(1)} %copy-done.5, f32[2,513,129]{2,1,0:T(8,128)} %get-tuple-element.21, f32[2,513,129]{2,1,0:T(8,128)S(1)} %get-tuple-element.20, f32[1,512,128]{2,1,0:T(8,128)S(1)} %bitcast.166, f32[1,512,128]{2,1,0:T(8,128)S(1)} %bitcast.165), kind=kLoop, calls=%fused_computation.72 | loop fusion | flops 917504 | bytes 3670016 | tf_op jit(solution)/shard_map/sub | solution.py:131
  (73 shorter events, 1.6 us)
Async XLA Ops:
  7.2 117.5 %copy-start = (bf16[8,128,128]{2,1,0:T(8,128)(2,1)S(1)}, bf16[8,128,128]{2,1,0:T(8,128)(2,1)}, u32[]{:S(2)}) copy-start(bf16[8,128,128]{2,1,0:T(8,128)(2,1)} %param.16) | copy-start | bytes 786436
  7.2 2.8 %copy-start.3 = (f32[2,512,128]{2,1,0:T(8,128)S(1)}, f32[2,512,128]{2,1,0:T(8,128)}, u32[]{:S(2)}) copy-start(f32[2,512,128]{2,1,0:T(8,128)} %param.10) | copy-start | bytes 1572868
  10.0 1.0 copy-start.8
  10.0 3.9 %copy-start.6 = (bf16[1,1024,2,256]{3,2,1,0:T(2,128)(2,1)}, bf16[1,1024,2,256]{3,2,1,0:T(2,128)(2,1)S(1)}, u32[]{:S(2)}) copy-start(bf16[1,1024,2,256]{3,2,1,0:T(2,128)(2,1)S(1)} %get-tuple-element.24) | copy-start | bytes 3145732
  13.3 1.2 copy-start.10
  17.7 66.7 %copy-start.20 = (u32[256]{0:T(256)S(1)}, u32[256]{0:T(256)}, u32[]{:S(2)}) copy-start(u32[256]{0:T(256)} %constant.75) | copy-start | bytes 3076
  85.8 11.9 %copy-start.15 = (s32[32,1,6]{0,1,2:T(1,128)S(1)}, s32[32,1,6]{0,1,2:T(1,128)}, u32[]{:S(2)}) copy-start(s32[32,1,6]{0,1,2:T(1,128)} %param.17) | copy-start | bytes 2308
  85.8 11.9 %copy-start.16 = (s32[32,1,6]{0,1,2:T(1,128)S(1)}, s32[32,1,6]{0,1,2:T(1,128)}, u32[]{:S(2)}) copy-start(s32[32,1,6]{0,1,2:T(1,128)} %param.18) | copy-start | bytes 2308
  85.8 12.0 %copy-start.19 = (s32[64]{0:T(128)S(1)}, s32[64]{0:T(128)}, u32[]{:S(2)}) copy-start(s32[64]{0:T(128)} %param.19) | copy-start | bytes 772
  87.6 35.5 %all-to-all-start = ((bf16[16,2,64,2,128]{4,1,3,2,0:T(2,128)(2,1)}), bf16[16,2,64,2,128]{4,1,3,2,0:T(2,128)(2,1)S(1)}, u32[]{:S(2)}, u32[]{:S(2)}) async-start(bf16[16,2,64,2,128]{4,1,3,2,0:T(2,128)(2,1)} %stack.23), calls=%async_computation | async-start | bytes 2097152 | tf_op jit(solution)/shard_map/all_to_all | solution.py:65
  97.6 90.4 %all-gather.3.cloned.1.call-start = ((), (), s32[]{:S(2)}) async-start(), calls=%async_computation.1 | async-start | bytes 2228224 | tf_op jit(solution)/shard_map/all_gather | solution.py:83
  124.3 1.0 copy-start.13
  124.3 1.0 copy-start.14
  125.3 2.4 copy-start.1
  127.6 99.2 %all-gather.5.cloned.1.call-start = ((), (), s32[]{:S(2)}) async-start(), calls=%async_computation.2 | async-start | bytes 1114112 | tf_op jit(solution)/shard_map/all_gather | solution.py:87
  131.2 9.9 %collective-permute-start = (f32[6,512,1]{1,2,0:T(1,128)S(1)}, f32[6,512,1]{1,2,0:T(1,128)S(1)}, u32[]{:S(2)}, u32[]{:S(2)}) collective-permute-start(f32[6,512,1]{1,2,0:T(1,128)S(1)} %copy.132), channel_id=1, source_target_pairs={{0,16},{16,32},{32,48},{48,64},{64,80},{80,96},{96,112},{112,128},... | collective-permute-start | bytes 36872 | tf_op jit(solution)/shard_map/ppermute | solution.py:16
  134.5 7.1 %collective-permute-start.1 = (f32[6,512,1]{1,2,0:T(1,128)S(1)}, f32[6,512,1]{1,2,0:T(1,128)S(1)}, u32[]{:S(2)}, u32[]{:S(2)}) collective-permute-start(f32[6,512,1]{1,2,0:T(1,128)S(1)} %copy.133), channel_id=1, source_target_pairs={{16,0},{32,16},{48,32},{64,48},{80,64},{96,80},{112,96},{128,112},... | collective-permute-start | bytes 36872 | tf_op jit(solution)/shard_map/ppermute | solution.py:19
  142.9 50.2 %collective-permute-start.2 = (f32[6,1,130]{2,1,0:T(1,128)S(1)}, f32[6,1,130]{2,1,0:T(1,128)S(1)}, u32[]{:S(2)}, u32[]{:S(2)}) collective-permute-start(f32[6,1,130]{2,1,0:T(1,128)S(1)} %get-tuple-element.19), channel_id=1, source_target_pairs={{0,1},{1,2},{2,3},{3,4},{4,5},{5,6},{6,7},{7,8},{8,9},{9,10},{10,1... | collective-permute-start | bytes 9368 | tf_op jit(solution)/shard_map/ppermute | solution.py:16
  145.0 48.2 %collective-permute-start.3 = (f32[6,1,130]{2,1,0:T(1,128)S(1)}, f32[6,1,130]{2,1,0:T(1,128)S(1)}, u32[]{:S(2)}, u32[]{:S(2)}) collective-permute-start(f32[6,1,130]{2,1,0:T(1,128)S(1)} %get-tuple-element.18), channel_id=1, source_target_pairs={{1,0},{2,1},{3,2},{4,3},{5,4},{6,5},{7,6},{8,7},{9,8},{10,9},{11,1... | collective-permute-start | bytes 9368 | tf_op jit(solution)/shard_map/ppermute | solution.py:19
  193.2 2.3 copy-start.2
  193.2 2.3 copy-start.4
  199.3 1.2 copy-start.12
  199.3 27.5 %copy-start.9 = (bf16[1,1024,2,256]{3,2,1,0:T(2,128)(2,1)S(1)}, bf16[1,1024,2,256]{3,2,1,0:T(2,128)(2,1)}, u32[]{:S(2)}) copy-start(bf16[1,1024,2,256]{3,2,1,0:T(2,128)(2,1)} %copy-done.8) | copy-start | bytes 3145732
  226.8 2.5 copy-start.7
  226.8 2.5 copy-start.17
  233.0 2.4 copy-start.18
  235.4 3.1 %copy-start.5 = (f32[2,512,128]{2,1,0:T(8,128)S(1)}, f32[2,512,128]{2,1,0:T(8,128)}, u32[]{:S(2)}) copy-start(f32[2,512,128]{2,1,0:T(8,128)} %param.10) | copy-start | bytes 1572868
  235.4 3.1 %copy-start.11 = (f32[2,256,128]{2,1,0:T(8,128)S(1)}, f32[2,256,128]{2,1,0:T(8,128)}, u32[]{:S(2)}) copy-start(f32[2,256,128]{2,1,0:T(8,128)} %copy.128) | copy-start | bytes 786436
Sparse Core Ops, SparseCore 0:
  127.7 60.2 all-gather.2
  193.1 33.6 all-gather.4
